TPU v7x, 512 devices: a whole 4x8x8 slice. The times are simulated.
512 devices in a mesh: req: 64 (over x, z, core), mdl: 8 (over y).
Axes of the slice: x: 4, y: 8, z: 8, core: 2. Of those that a mesh axis runs over, the one named last changes fastest.
Arguments:
- queries: bfloat16 [1536, 2048], P('req', 'mdl'), may hold values from -6 to 6
- scored_key_value: bfloat16 [2, 1536, 1024], P(None, 'req', 'mdl'), may hold values from -6 to 6
- gate_logits: bfloat16 [1536, 2048], P('req', 'mdl'), may hold values from -8 to 8
- page_kv: bfloat16 [2, 2176, 128, 1024], P(None, 'req', None, 'mdl'), may hold values from -6 to 6
- page_table: int32 [64, 128], replicated, may hold values from -1 to 2175, as said below
- lengths: int32 [64], replicated, may hold values from 1 to 16384
- assignment: int32 [64], replicated, may hold values from 0 to 63, each once
- offsets: int32 [64, 24], P('req'), may hold values from 0 to 23, each once within a row
- residual: bfloat16 [1536, 2048], P('req'), may hold values from -18 to 18
- out_weight: bfloat16 [2048, 2048], P('mdl'), may hold values from -1 to 1
- norm_gain: bfloat16 [2048], replicated, may hold values from 0.5 to 1.5
- head_weight: bfloat16 [2048, 131072], P(None, ('req', 'mdl')), may hold values from -0.3193592 to 0.3193592
- targets: int32 [1536], replicated, may hold values from 0 to 131071
Outputs:
- logprob: float32 [1536], P('req')
- entropy: float32 [1536], P('req')
Inputs may be any that keep to these rules, and one draw needn't show every extreme that they name: `page_table`: row i lists the pages of request i in order, each as owner index times 34 plus a slot, followed by -1. Request i has ceil(lengths[i] / 128) pages, no page serves two requests, and at most 2 pages of one request sit on one owner. `assignment`: each index along req holds exactly one request. `offsets`: each row is an order of 0 to 23.
All inputs are finite; a program needn't handle non-finite values.
Results may differ from a plain program's by a relative error of at most 0.0013.
Values may be sent and summed in bfloat16 or wider, within the bound.
No kernel may reach another device: no remote copies, remote signals or barrier semaphores. Data moves between devices by JAX's collectives and lax.ppermute only.
A program may use at most 128 MiB of HBM per device.

v0:
```python
import jax
import jax.numpy as jnp
from jax import lax
from jax.sharding import PartitionSpec as P

HEAD_SIZE = 128
CAP = 2
FLOOR_SCORE = -1e30
NORM_EPSILON = 1e-06


def merge_stats(parts):
    peak = jnp.max(parts[:, :, 0], axis=0)
    scale = jnp.exp(parts[:, :, 0] - peak[None])
    total = jnp.sum(parts[:, :, 1] * scale, axis=0)
    moment = jnp.sum(parts[:, :, 2] * scale, axis=0)
    chosen = jnp.sum(parts[:, :, 3], axis=0)
    return jnp.stack([peak, total, moment, chosen], axis=1)


def body(
    queries,
    scored_key_value,
    gate_logits,
    page_kv,
    page_table,
    lengths,
    assignment,
    offsets,
    residual,
    out_weight,
    norm_gain,
    head_weight,
    targets,
):
    groups = lax.axis_size("req")
    req_index = lax.axis_index("req")
    fresh_count = queries.shape[0]
    kv_heads = scored_key_value.shape[2] // HEAD_SIZE
    queries_per_group = queries.shape[1] // scored_key_value.shape[2]
    page_len = page_kv.shape[2]
    store_pages = page_kv.shape[1]
    page_slots = page_table.shape[1]
    score_scale = HEAD_SIZE ** (-0.5)
    indices = jnp.arange(groups, dtype=jnp.int32)
    holder = jnp.sum(
        jnp.where(assignment[:, None] == indices[None, :], indices[:, None], 0), axis=0
    )
    query_heads = queries.reshape(fresh_count, kv_heads, queries_per_group, HEAD_SIZE)
    scored_keys = scored_key_value[0].reshape(fresh_count, kv_heads, HEAD_SIZE)
    scored_values = scored_key_value[1].reshape(fresh_count, kv_heads, HEAD_SIZE)
    fresh_order = offsets[0]
    visible = fresh_order[None, :] <= fresh_order[:, None]
    fresh_scores = (
        jnp.einsum("tjgd,ujd->jgtu", query_heads, scored_keys, preferred_element_type=jnp.float32)
        * score_scale
    )
    fresh_scores = jnp.where(visible[None, None], fresh_scores, FLOOR_SCORE)
    fresh_top = jnp.max(fresh_scores, axis=-1)
    page_owner = jnp.where(page_table >= 0, page_table // store_pages, -1)
    page_slot = page_table % store_pages
    is_mine = page_owner == req_index
    page_rank = jnp.cumsum(is_mine.astype(jnp.int32), axis=1) - 1
    slot_picks = [
        jnp.sum(jnp.where(is_mine & (page_rank == cap_index), page_slot, 0), axis=1)
        for cap_index in range(CAP)
    ]
    send_slot = jnp.take(jnp.stack(slot_picks, axis=1), holder, axis=0).reshape(-1)
    outgoing = jnp.take(page_kv, send_slot, axis=1)
    arrived = lax.all_to_all(outgoing, "req", split_axis=1, concat_axis=1, tiled=True)
    request = holder[req_index]
    page_table_row = jnp.take(page_table, request, axis=0)
    length = jnp.take(lengths, request)
    row_owner = jnp.where(page_table_row >= 0, page_table_row // store_pages, -1)
    source = row_owner[None, :] == indices[:, None]
    row_rank = jnp.cumsum(source.astype(jnp.int32), axis=1) - 1
    page_fill = jnp.clip(length - jnp.arange(page_slots, dtype=jnp.int32) * page_len, 0, page_len)
    counts = jnp.stack(
        [
            jnp.sum(jnp.where(source & (row_rank == cap_index), page_fill[None, :], 0), axis=1)
            for cap_index in range(CAP)
        ],
        axis=1,
    ).reshape(-1)
    live_keys = (jnp.arange(page_len, dtype=jnp.int32)[None, :] < counts[:, None]).reshape(-1)
    cached_keys = arrived[0].reshape(-1, kv_heads, HEAD_SIZE)
    cached_values = arrived[1].reshape(-1, kv_heads, HEAD_SIZE)
    scores = (
        jnp.einsum("tjgd,ljd->jgtl", query_heads, cached_keys, preferred_element_type=jnp.float32)
        * score_scale
    )
    scores = jnp.where(live_keys[None, None, None, :], scores, FLOOR_SCORE)
    row_top = jnp.maximum(jnp.max(scores, axis=-1), fresh_top)
    weights = jnp.exp(scores - row_top[..., None])
    weight_sum = jnp.sum(weights, axis=-1)
    summed = jnp.einsum(
        "jgtl,ljd->tjgd",
        weights.astype(jnp.bfloat16),
        cached_values,
        preferred_element_type=jnp.float32,
    )
    fresh_weights = jnp.exp(fresh_scores - row_top[..., None])
    weight_sum = weight_sum + jnp.sum(fresh_weights, axis=-1)
    summed = summed + jnp.einsum(
        "jgtu,ujd->tjgd",
        fresh_weights.astype(jnp.bfloat16),
        scored_values,
        preferred_element_type=jnp.float32,
    )
    attended = summed / jnp.transpose(weight_sum, (2, 0, 1))[..., None]
    gated_out = (
        attended.reshape(fresh_count, -1) * jax.nn.sigmoid(gate_logits.astype(jnp.float32))
    ).astype(jnp.bfloat16)
    update = lax.psum(jnp.dot(gated_out, out_weight, preferred_element_type=jnp.float32), "mdl")
    stream = residual.astype(jnp.float32) + update
    normed = (
        stream
        * lax.rsqrt(jnp.mean(stream * stream, axis=-1, keepdims=True) + NORM_EPSILON)
        * norm_gain.astype(jnp.float32)
    ).astype(jnp.bfloat16)
    logits = jnp.dot(
        lax.all_gather(normed, "req", axis=0, tiled=True),
        head_weight,
        preferred_element_type=jnp.float32,
    )
    vocab_width = head_weight.shape[1]
    mdl_size = lax.axis_size("mdl")
    mdl_index = lax.axis_index("mdl")
    vocab_start = (req_index * mdl_size + mdl_index) * vocab_width
    columns = vocab_start + jnp.arange(vocab_width, dtype=jnp.int32)
    chosen = jnp.sum(jnp.where(targets[:, None] == columns[None, :], logits, 0.0), axis=1)
    local_peak = jnp.max(logits, axis=1)
    local_weights = jnp.exp(logits - local_peak[:, None])
    stats = jnp.stack(
        [
            local_peak,
            jnp.sum(local_weights, axis=1),
            jnp.sum(local_weights * logits, axis=1),
            chosen,
        ],
        axis=1,
    ).reshape(groups, fresh_count, 4)
    stats = lax.all_to_all(stats, "req", 0, 0, tiled=True)
    stats = merge_stats(stats)
    slots = jnp.where(
        (jnp.arange(mdl_size, dtype=jnp.int32) == mdl_index)[:, None, None], stats[None], 0.0
    )
    stats = merge_stats(lax.psum(slots, "mdl"))
    row_peak, vocab_total, moment, chosen = (stats[:, i] for i in range(4))
    log_total = row_peak + jnp.log(vocab_total)
    logprob = chosen - log_total
    entropy = log_total - moment / vocab_total
    return (logprob, entropy)


def solution(mesh):
    placed = (
        P("req", "mdl"),
        P(None, "req", "mdl"),
        P("req", "mdl"),
        P(None, "req", None, "mdl"),
        P(),
        P(),
        P(),
        P("req", None),
        P("req", None),
        P("mdl", None),
        P(),
        P(None, ("req", "mdl")),
        P(),
    )
    return jax.shard_map(
        body, mesh=mesh, in_specs=placed, out_specs=(P("req"), P("req")), check_vma=False
    )
```

profile of v0, /device:TPU:2, one launch (start us, length us, event | category | flops | bytes accessed | tf_op | source)
XLA Modules:
  0.0 460.2 jit_solution(17138256541954221748)
XLA Ops:
  7.2 0.9 select_reduce_fusion.5
  8.1 0.8 fusion.57
  9.2 0.9 select_reduce_fusion.4
  10.2 0.6 gather_fusion
  11.2 6.4 %gather_fusion.1 = bf16[128,2,128,128]{3,2,1,0:T(8,128)(2,1)} fusion(bf16[2,34,128,128]{3,2,1,0:T(8,128)(2,1)S(1)} %copy-done, s32[1024]{0:T(1024)S(1)} %pad_clamp_fusion), kind=kCustom, calls=%fused_computation.1 | custom fusion | bytes 16777728 | tf_op jit(solution)/shard_map/jit(_take)/gather | solution.py:69
  17.6 7.4 %select_bitcast_fusion = bf16[2,128,128,128]{3,2,0,1:T(8,128)(2,1)} fusion(bf16[128,2,128,128]{3,2,1,0:T(8,128)(2,1)} %gather_fusion.1, pred[128]{0:T(512)(128)(4,1)S(1)} %compare_and_fusion), kind=kLoop, calls=%fused_computation.6 | loop fusion | flops 4194304 | bytes 16777344 | tf_op jit(solution)/shard_map/jit(_take)/select_n | solution.py:69
  25.0 14.2 %all-to-all-start = ((bf16[2,128,128,128]{3,2,0,1:T(8,128)(2,1)}), bf16[2,128,128,128]{3,2,0,1:T(8,128)(2,1)}, u32[]{:S(2)}, u32[]{:S(2)}) async-start(bf16[2,128,128,128]{3,2,0,1:T(8,128)(2,1)} %select_bitcast_fusion), calls=%async_computation | async-start | bytes 16777216 | tf_op jit(solution)/shard_map/all_to_all | solution.py:70
  43.1 0.7 bitcast_select_fusion.1
  44.8 178.7 %all-to-all-done = bf16[2,128,128,128]{3,2,0,1:T(8,128)(2,1)} async-done(((bf16[2,128,128,128]{3,2,0,1:T(8,128)(2,1)}), bf16[2,128,128,128]{3,2,0,1:T(8,128)(2,1)}, u32[]{:S(2)}, u32[]{:S(2)}) %all-to-all-start) | async-done | bytes 8388640 | tf_op jit(solution)/shard_map/all_to_all | solution.py:70
  223.5 4.0 fusion.58
  227.5 2.7 fusion.60
  230.4 0.7 fusion.3
  231.2 1.0 fusion.16
  232.4 0.9 fusion.33
  233.4 76.0 %all-reduce.2.cloned.1.call-done = f32[24,2048]{1,0:T(8,128)} async-done(((f32[24,2048]{1,0:T(8,128)}), f32[24,2048]{1,0:T(8,128)}) %all-reduce.2.cloned.1.call-update) | async-done | bytes 196624 | tf_op jit(solution)/shard_map/psum | solution.py:114
  309.4 1.1 multiply_reduce_fusion.1
  310.5 1.6 multiply_convert_fusion
  312.2 84.7 %all-gather.2.cloned.1.call-done = bf16[1536,2048]{1,0:T(8,128)(2,1)} async-done(((bf16[24,2048]{1,0:T(8,128)(2,1)}), bf16[1536,2048]{1,0:T(8,128)(2,1)}) %all-gather.2.cloned.1.call-update) | async-done | bytes 6291472 | tf_op jit(solution)/shard_map/all_gather | solution.py:122
  396.9 5.8 %fusion.62 = (f32[1536]{0:T(1024)S(1)}, f32[1536,256]{0,1:T(8,128)}) fusion(bf16[1536,2048]{1,0:T(8,128)(2,1)} %all-gather.2.cloned.1.call-done, bf16[2048,256]{1,0:T(8,128)(2,1)S(1)} %copy-done.9), kind=kOutput, calls=%fused_computation.115 | convolution fusion | flops 1611004416 | bytes 8919040 | tf_op jit(solution)/shard_map/dot_general | solution.py:121
  402.7 1.9 fusion.8
  404.9 0.7 copy.55
  405.6 7.4 %all-to-all-start.1 = ((f32[64,24,4]{1,2,0:T(4,128)}), f32[64,24,4]{1,2,0:T(4,128)S(1)}, u32[]{:S(2)}, u32[]{:S(2)}) async-start(f32[64,24,4]{1,2,0:T(4,128)} %copy.55), calls=%async_computation.1 | async-start | bytes 262144 | tf_op jit(solution)/shard_map/all_to_all | solution.py:143
  413.1 9.4 %all-to-all-done.1 = f32[64,24,4]{1,2,0:T(4,128)S(1)} async-done(((f32[64,24,4]{1,2,0:T(4,128)}), f32[64,24,4]{1,2,0:T(4,128)S(1)}, u32[]{:S(2)}, u32[]{:S(2)}) %all-to-all-start.1) | async-done | bytes 24608 | tf_op jit(solution)/shard_map/all_to_all | solution.py:143
  423.0 29.7 %psum.15 = f32[8,24,4]{1,0,2:T(8,128)S(1)} all-reduce(f32[8,24,4]{1,0,2:T(8,128)S(1)} %broadcast_select_fusion.1), channel_id=1, replica_groups=mesh['req'=64,'mdl'=8] {'mdl'}, use_global_device_ids=true, to_apply=%region_21.22 | all-reduce | flops 768 | bytes 6144 | tf_op jit(solution)/shard_map/psum | solution.py:148
  (73 shorter events, 5.1 us)
Async XLA Ops:
  7.2 4.1 copy-start
  25.0 16.8 %copy-start.10 = (s32[64]{0:T(128)S(1)}, s32[64]{0:T(128)}, u32[]{:S(2)}) copy-start(s32[64]{0:T(128)} %param.18) | copy-start | bytes 772
  25.0 19.5 %copy-start.8 = (s32[1,24]{1,0:T(1,128)S(1)}, s32[1,24]{1,0:T(1,128)}, u32[]{:S(2)}) copy-start(s32[1,24]{1,0:T(1,128)} %param.20) | copy-start | bytes 292
  25.0 19.5 %copy-start.3 = (bf16[24,256]{1,0:T(8,128)(2,1)S(1)}, bf16[24,256]{1,0:T(8,128)(2,1)}, u32[]{:S(2)}) copy-start(bf16[24,256]{1,0:T(8,128)(2,1)} %param.13) | copy-start | bytes 36868
  25.0 19.5 %copy-start.7 = (bf16[2,24,128]{2,1,0:T(8,128)(2,1)S(1)}, bf16[2,24,128]{2,1,0:T(8,128)(2,1)}, u32[]{:S(2)}) copy-start(bf16[2,24,128]{2,1,0:T(8,128)(2,1)} %param.14) | copy-start | bytes 36868
  25.0 198.5 %all-to-all-start = ((bf16[2,128,128,128]{3,2,0,1:T(8,128)(2,1)}), bf16[2,128,128,128]{3,2,0,1:T(8,128)(2,1)}, u32[]{:S(2)}, u32[]{:S(2)}) async-start(bf16[2,128,128,128]{3,2,0,1:T(8,128)(2,1)} %select_bitcast_fusion), calls=%async_computation | async-start | bytes 16777216 | tf_op jit(solution)/shard_map/all_to_all | solution.py:70
  39.2 270.2 %all-reduce.2.cloned.1.call-start = ((), (), s32[]{:S(2)}) async-start(), calls=%async_computation.2 | async-start | bytes 393216 | tf_op jit(solution)/shard_map/psum | solution.py:114
  231.1 1.2 copy-start.1
  231.1 1.2 copy-start.4
  231.1 2.2 copy-start.6
  231.1 78.3 %copy-start.2 = (bf16[24,2048]{1,0:T(8,128)(2,1)S(1)}, bf16[24,2048]{1,0:T(8,128)(2,1)}, u32[]{:S(2)}) copy-start(bf16[24,2048]{1,0:T(8,128)(2,1)} %param.21) | copy-start | bytes 294916
  231.2 165.7 %copy-start.9 = (bf16[2048,256]{1,0:T(8,128)(2,1)S(1)}, bf16[2048,256]{1,0:T(8,128)(2,1)}, u32[]{:S(2)}) copy-start(bf16[2048,256]{1,0:T(8,128)(2,1)} %param.24) | copy-start | bytes 3145732
  233.3 163.5 %all-gather.2.cloned.1.call-start = ((), (), s32[]{:S(2)}) async-start(), calls=%async_computation.3 | async-start | bytes 6389760 | tf_op jit(solution)/shard_map/all_gather | solution.py:122
  312.2 90.6 %copy-start.5 = (s32[1536]{0:T(1024)S(1)}, s32[1536]{0:T(1024)}, u32[]{:S(2)}) copy-start(s32[1536]{0:T(1024)} %param.25) | copy-start | bytes 18436
  405.6 16.8 %all-to-all-start.1 = ((f32[64,24,4]{1,2,0:T(4,128)}), f32[64,24,4]{1,2,0:T(4,128)S(1)}, u32[]{:S(2)}, u32[]{:S(2)}) async-start(f32[64,24,4]{1,2,0:T(4,128)} %copy.55), calls=%async_computation.1 | async-start | bytes 262144 | tf_op jit(solution)/shard_map/all_to_all | solution.py:143
Sparse Core Ops, SparseCore 0:
  233.4 75.9 all-reduce.1
  312.7 84.0 all-gather.1
where the time goes:
time: 461 us; the launch traced here: 460 us
  waiting for transfers between devices  349 us (76%)
  blocking collectives  29.7 us (6%)
  starting transfers between devices  21.7 us (5%)
  other arithmetic  18.1 us (4%)
  between operations  16.9 us (4%)
  local copies, waits for them, and re-layouts  14.3 us (3%)
  matrix products  10.7 us (2%)
    all_to_all x1, waiting for transfers between devices, body(): lax.all_to_all(outgoing, 'req', split_axis=1, concat_axis=1, tiled=True)  179 us
    all_gather x1, waiting for transfers between devices, body(): lax.all_gather(normed, 'req', axis=0, tiled=True)  84.7 us
    psum x1, waiting for transfers between devices, body(): lax.psum(jnp.dot(gated_out, out_weight, preferred_element_type=jnp.float3...  76 us
    psum x1, blocking collectives, body(): stats = merge_stats(lax.psum(slots, 'mdl'))  29.7 us
    all_to_all x1, starting transfers between devices, body(): lax.all_to_all(outgoing, 'req', split_axis=1, concat_axis=1, tiled=True)  14.2 us
    all_to_all x1, waiting for transfers between devices, body(): stats = lax.all_to_all(stats, 'req', 0, 0, tiled=True)  9.35 us
  transfers between devices with their start and end apart: 4, of which 4 were waited for; matrix products, arithmetic and copies ran while one was open for 1% of the time, Pallas kernels for 0%

commit v1 on v0

--- a/solution.py
+++ b/solution.py
@@ -119,7 +119,9 @@
         * norm_gain.astype(jnp.float32)
     ).astype(jnp.bfloat16)
     logits = jnp.dot(
-        lax.all_gather(normed, "req", axis=0, tiled=True),
+        jnp.concatenate(
+            lax.all_to_all(jnp.stack([normed] * lax.axis_size("req")), "req", 0, 0), axis=0
+        ),
         head_weight,
         preferred_element_type=jnp.float32,
     )

time: 461 us -> 529 us (1.15)
  waiting for transfers between devices: 349 us -> 404 us
  starting transfers between devices: 21.7 us -> 32.6 us
    all_to_all x0 -> x1, waiting for transfers between devices: none -> 139 us  [body(): lax.all_to_all(jnp.stack([normed] * lax.axis_size('req')), 'req', 0, 0)]
    all_gather x1 -> x0, waiting for transfers between devices: 84.7 us -> none  [body(): lax.all_gather(normed, 'req', axis=0, tiled=True)]
    all_to_all x0 -> x1, starting transfers between devices: none -> 11.2 us  [body(): lax.all_to_all(jnp.stack([normed] * lax.axis_size('req')), 'req', 0, 0)]
where the time goes in v1:
time: 529 us; the launch traced here: 528 us
  waiting for transfers between devices  404 us (76%)
  starting transfers between devices  32.6 us (6%)
  blocking collectives  29.1 us (6%)
  local copies, waits for them, and re-layouts  17.7 us (3%)
  other arithmetic  17.5 us (3%)
  between operations  16.9 us (3%)
  matrix products  10.7 us (2%)
    all_to_all x1, waiting for transfers between devices, body(): lax.all_to_all(outgoing, 'req', split_axis=1, concat_axis=1, tiled=True)  179 us
    all_to_all x1, waiting for transfers between devices, body(): lax.all_to_all(jnp.stack([normed] * lax.axis_size('req')), 'req', 0, 0)  139 us
    psum x1, waiting for transfers between devices, body(): lax.psum(jnp.dot(gated_out, out_weight, preferred_element_type=jnp.float3...  76.1 us
    psum x1, blocking collectives, body(): stats = merge_stats(lax.psum(slots, 'mdl'))  29.1 us
    all_to_all x1, starting transfers between devices, body(): lax.all_to_all(outgoing, 'req', split_axis=1, concat_axis=1, tiled=True)  14.2 us
    all_to_all x1, starting transfers between devices, body(): lax.all_to_all(jnp.stack([normed] * lax.axis_size('req')), 'req', 0, 0)  11.2 us
  transfers between devices with their start and end apart: 4, of which 4 were waited for; matrix products, arithmetic and copies ran while one was open for 1% of the time, Pallas kernels for 0%

profile of v1, /device:TPU:2, one launch (start us, length us, event | category | flops | bytes accessed | tf_op | source)
XLA Modules:
  0.0 528.1 jit_solution(6320056742321499790)
XLA Ops:
  7.2 0.9 select_reduce_fusion.5
  8.1 0.8 fusion.57
  9.2 0.9 select_reduce_fusion.4
  11.2 6.4 %gather_fusion.1 = bf16[128,2,128,128]{3,2,1,0:T(8,128)(2,1)} fusion(bf16[2,34,128,128]{3,2,1,0:T(8,128)(2,1)S(1)} %copy-done, s32[1024]{0:T(1024)S(1)} %pad_clamp_fusion), kind=kCustom, calls=%fused_computation.1 | custom fusion | bytes 16777728 | tf_op jit(solution)/shard_map/jit(_take)/gather | solution.py:69
  17.6 7.4 %select_bitcast_fusion = bf16[2,128,128,128]{3,2,0,1:T(8,128)(2,1)} fusion(bf16[128,2,128,128]{3,2,1,0:T(8,128)(2,1)} %gather_fusion.1, pred[128]{0:T(512)(128)(4,1)S(1)} %compare_and_fusion), kind=kLoop, calls=%fused_computation.6 | loop fusion | flops 4194304 | bytes 16777344 | tf_op jit(solution)/shard_map/jit(_take)/select_n | solution.py:69
  25.0 14.2 %all-to-all-start = ((bf16[2,128,128,128]{3,2,0,1:T(8,128)(2,1)}), bf16[2,128,128,128]{3,2,0,1:T(8,128)(2,1)}, u32[]{:S(2)}, u32[]{:S(2)}) async-start(bf16[2,128,128,128]{3,2,0,1:T(8,128)(2,1)} %select_bitcast_fusion), calls=%async_computation | async-start | bytes 16777216 | tf_op jit(solution)/shard_map/all_to_all | solution.py:70
  44.8 178.7 %all-to-all-done = bf16[2,128,128,128]{3,2,0,1:T(8,128)(2,1)} async-done(((bf16[2,128,128,128]{3,2,0,1:T(8,128)(2,1)}), bf16[2,128,128,128]{3,2,0,1:T(8,128)(2,1)}, u32[]{:S(2)}, u32[]{:S(2)}) %all-to-all-start) | async-done | bytes 8388640 | tf_op jit(solution)/shard_map/all_to_all | solution.py:70
  223.5 4.0 fusion.58
  227.5 2.7 fusion.60
  230.4 0.7 fusion.3
  231.2 1.0 fusion.16
  232.4 0.9 fusion.33
  233.3 76.1 %all-reduce.2.cloned.1.call-done = f32[24,2048]{1,0:T(8,128)} async-done(((f32[24,2048]{1,0:T(8,128)}), f32[24,2048]{1,0:T(8,128)}) %all-reduce.2.cloned.1.call-update) | async-done | bytes 196624 | tf_op jit(solution)/shard_map/psum | solution.py:114
  309.4 1.1 multiply_reduce_fusion.1
  310.5 1.0 multiply_convert_fusion
  311.5 3.4 stack.40
  315.0 11.2 %all-to-all-start.1 = ((bf16[64,24,2048]{2,1,0:T(8,128)(2,1)}), bf16[64,24,2048]{2,1,0:T(8,128)(2,1)}, u32[]{:S(2)}, u32[]{:S(2)}) async-start(bf16[64,24,2048]{2,1,0:T(8,128)(2,1)} %stack.40), calls=%async_computation.1 | async-start | bytes 12582912 | tf_op jit(solution)/shard_map/all_to_all | solution.py:123
  326.2 139.5 %all-to-all-done.1 = bf16[64,24,2048]{2,1,0:T(8,128)(2,1)} async-done(((bf16[64,24,2048]{2,1,0:T(8,128)(2,1)}), bf16[64,24,2048]{2,1,0:T(8,128)(2,1)}, u32[]{:S(2)}, u32[]{:S(2)}) %all-to-all-start.1) | async-done | bytes 6291488 | tf_op jit(solution)/shard_map/all_to_all | solution.py:123
  465.7 5.8 %fusion.62 = (f32[1536]{0:T(1024)S(1)}, f32[1536,256]{0,1:T(8,128)}) fusion(bf16[1536,2048]{1,0:T(8,128)(2,1)} %bitcast.35, bf16[2048,256]{1,0:T(8,128)(2,1)S(1)} %copy-done.9), kind=kOutput, calls=%fused_computation.115 | convolution fusion | flops 1611004416 | bytes 8919040 | tf_op jit(solution)/shard_map/dot_general | solution.py:121
  471.6 1.9 fusion.8
  473.8 0.7 copy.55
  474.5 7.1 %all-to-all-start.2 = ((f32[64,24,4]{1,2,0:T(4,128)}), f32[64,24,4]{1,2,0:T(4,128)S(1)}, u32[]{:S(2)}, u32[]{:S(2)}) async-start(f32[64,24,4]{1,2,0:T(4,128)} %copy.55), calls=%async_computation.2 | async-start | bytes 262144 | tf_op jit(solution)/shard_map/all_to_all | solution.py:145
  481.6 9.4 %all-to-all-done.2 = f32[64,24,4]{1,2,0:T(4,128)S(1)} async-done(((f32[64,24,4]{1,2,0:T(4,128)}), f32[64,24,4]{1,2,0:T(4,128)S(1)}, u32[]{:S(2)}, u32[]{:S(2)}) %all-to-all-start.2) | async-done | bytes 24608 | tf_op jit(solution)/shard_map/all_to_all | solution.py:145
  491.6 29.1 %psum.15 = f32[8,24,4]{1,0,2:T(8,128)S(1)} all-reduce(f32[8,24,4]{1,0,2:T(8,128)S(1)} %broadcast_select_fusion.1), channel_id=1, replica_groups=mesh['req'=64,'mdl'=8] {'mdl'}, use_global_device_ids=true, to_apply=%region_21.22 | all-reduce | flops 768 | bytes 6144 | tf_op jit(solution)/shard_map/psum | solution.py:150
  (73 shorter events, 6.4 us)
Async XLA Ops:
  7.2 4.1 copy-start
  25.0 16.8 %copy-start.10 = (s32[64]{0:T(128)S(1)}, s32[64]{0:T(128)}, u32[]{:S(2)}) copy-start(s32[64]{0:T(128)} %param.18) | copy-start | bytes 772
  25.0 19.5 %copy-start.8 = (s32[1,24]{1,0:T(1,128)S(1)}, s32[1,24]{1,0:T(1,128)}, u32[]{:S(2)}) copy-start(s32[1,24]{1,0:T(1,128)} %param.20) | copy-start | bytes 292
  25.0 19.5 %copy-start.3 = (bf16[24,256]{1,0:T(8,128)(2,1)S(1)}, bf16[24,256]{1,0:T(8,128)(2,1)}, u32[]{:S(2)}) copy-start(bf16[24,256]{1,0:T(8,128)(2,1)} %param.13) | copy-start | bytes 36868
  25.0 19.5 %copy-start.7 = (bf16[2,24,128]{2,1,0:T(8,128)(2,1)S(1)}, bf16[2,24,128]{2,1,0:T(8,128)(2,1)}, u32[]{:S(2)}) copy-start(bf16[2,24,128]{2,1,0:T(8,128)(2,1)} %param.14) | copy-start | bytes 36868
  25.0 198.5 %all-to-all-start = ((bf16[2,128,128,128]{3,2,0,1:T(8,128)(2,1)}), bf16[2,128,128,128]{3,2,0,1:T(8,128)(2,1)}, u32[]{:S(2)}, u32[]{:S(2)}) async-start(bf16[2,128,128,128]{3,2,0,1:T(8,128)(2,1)} %select_bitcast_fusion), calls=%async_computation | async-start | bytes 16777216 | tf_op jit(solution)/shard_map/all_to_all | solution.py:70
  39.2 270.2 %all-reduce.2.cloned.1.call-start = ((), (), s32[]{:S(2)}) async-start(), calls=%async_computation.3 | async-start | bytes 393216 | tf_op jit(solution)/shard_map/psum | solution.py:114
  231.1 1.2 copy-start.1
  231.1 1.2 copy-start.4
  231.1 2.2 copy-start.6
  231.1 78.3 %copy-start.2 = (bf16[24,2048]{1,0:T(8,128)(2,1)S(1)}, bf16[24,2048]{1,0:T(8,128)(2,1)}, u32[]{:S(2)}) copy-start(bf16[24,2048]{1,0:T(8,128)(2,1)} %param.21) | copy-start | bytes 294916
  315.0 150.7 %copy-start.9 = (bf16[2048,256]{1,0:T(8,128)(2,1)S(1)}, bf16[2048,256]{1,0:T(8,128)(2,1)}, u32[]{:S(2)}) copy-start(bf16[2048,256]{1,0:T(8,128)(2,1)} %param.24) | copy-start | bytes 3145732
  315.0 150.7 %all-to-all-start.1 = ((bf16[64,24,2048]{2,1,0:T(8,128)(2,1)}), bf16[64,24,2048]{2,1,0:T(8,128)(2,1)}, u32[]{:S(2)}, u32[]{:S(2)}) async-start(bf16[64,24,2048]{2,1,0:T(8,128)(2,1)} %stack.40), calls=%async_computation.1 | async-start | bytes 12582912 | tf_op jit(solution)/shard_map/all_to_all | solution.py:123
  465.7 5.9 %copy-start.5 = (s32[1536]{0:T(1024)S(1)}, s32[1536]{0:T(1024)}, u32[]{:S(2)}) copy-start(s32[1536]{0:T(1024)} %param.25) | copy-start | bytes 18436
  474.5 16.5 %all-to-all-start.2 = ((f32[64,24,4]{1,2,0:T(4,128)}), f32[64,24,4]{1,2,0:T(4,128)S(1)}, u32[]{:S(2)}, u32[]{:S(2)}) async-start(f32[64,24,4]{1,2,0:T(4,128)} %copy.55), calls=%async_computation.2 | async-start | bytes 262144 | tf_op jit(solution)/shard_map/all_to_all | solution.py:145
Sparse Core Ops, SparseCore 0:
  233.4 75.9 all-reduce.1
